TPU v7x, 512 devices: a whole 4x8x8 slice. The times are simulated.
512 devices in a mesh: ctx: 128 (over y, z, core), tp: 4 (over x).
Axes of the slice: x: 4, y: 8, z: 8, core: 2. Of those that a mesh axis runs over, the one named last changes fastest.
Arguments:
- hidden_in: bfloat16 [16384, 1536], P('ctx', 'tp'), may hold values from -60 to 60
- queries: bfloat16 [16384, 2048], P('ctx', 'tp'), may hold values from -200 to 200
- rotated_key_value: bfloat16 [16384, 4, 128], P('ctx', 'tp'), may hold values from -5 to 5
- sink_logit_table: float32 [32], P('tp'), may hold values from -2 to 2
- out_proj: bfloat16 [2048, 1536], P('tp', 'ctx'), may hold values from -0.125 to 0.125
- norm_gain: float32 [1536], P('tp'), may hold values from 0.1 to 1.9
- expert_in: bfloat16 [128, 2, 1536, 1536], P('ctx', None, None, 'tp'), may hold values from -0.15625 to 0.15625
- expert_out: bfloat16 [128, 1536, 1536], P('ctx', 'tp'), may hold values from -0.15625 to 0.15625
- routes: int32 [16384, 4], P('ctx'), may hold values from 0 to 127, all different within a row; in each aligned block of 128 rows (0 to 127, 128 to 255, ...) at most 12 rows name the same one
- route_scores: float32 [16384, 4], P('ctx'), may hold values from 0.05 to 1
Outputs:
- layer_out: bfloat16 [16384, 1536], P('ctx', 'tp')
Inputs may be any that keep to these rules, and one draw needn't show every extreme that they name: `routes`: each token names 4 different experts. In every aligned block of 128 tokens (the tokens of one device) no expert is named by more than 12 tokens, a bound that some block reaches.
All inputs are finite; a program needn't handle non-finite values.
Results may differ from a plain program's by a relative error of at most 0.008.
Values may be sent and summed in bfloat16 or wider, within the bound.
No kernel may reach another device: no remote copies, remote signals or barrier semaphores. Data moves between devices by JAX's collectives and lax.ppermute only.
A program may use at most 64 MiB of HBM per device.

v0:
```python
import jax
import jax.numpy as jnp
from jax import lax
from jax.sharding import PartitionSpec as P

WINDOW_KEYS = 128


def shifted(value, axis, steps):
    count = lax.axis_size(axis)
    first, last = (max(0, -steps), min(count, count - steps))
    return lax.ppermute(value, axis, [(source, source + steps) for source in range(first, last)])


def attend(query_block, key_blk, value_blk, inside, sink_row_block, factor):
    score = (
        jnp.einsum("rgqd,sgd->gqrs", query_block, key_blk, preferred_element_type=jnp.float32)
        * factor
    )
    masked = jnp.where(inside, score, -1e30)
    top_score = jnp.maximum(jnp.max(masked, -1), sink_row_block[:, :, None])
    expvals = jnp.where(inside, jnp.exp(score - top_score[..., None]), 0.0)
    denominator = jnp.sum(expvals, -1) + jnp.exp(sink_row_block[:, :, None] - top_score)
    probs = (expvals / denominator[..., None]).astype(jnp.bfloat16)
    mixed = jnp.einsum("gqrs,sgd->rgqd", probs, value_blk, preferred_element_type=jnp.float32)
    return mixed.astype(jnp.bfloat16)


def body(
    hidden_in,
    queries,
    rotated_key_value,
    sink_logit_table,
    out_proj,
    norm_gain,
    expert_in,
    expert_out,
    routes,
    route_scores,
):
    tok_rows = hidden_in.shape[0]
    kv_heads = rotated_key_value.shape[1]
    head_dim = rotated_key_value.shape[2] // 2
    q_heads = sink_logit_table.shape[0]
    queries_per_group = q_heads // kv_heads
    factor = head_dim ** (-0.5)
    sink_row_block = sink_logit_table.reshape(kv_heads, queries_per_group)
    earlier = shifted(rotated_key_value, "ctx", 1)
    keys_all = jnp.concatenate([earlier, rotated_key_value], 0)
    first_pos = lax.axis_index("ctx") * tok_rows
    block_row_count = min(512, tok_rows)
    query_block = queries.reshape(block_row_count, kv_heads, queries_per_group, head_dim)
    query_pos = first_pos + 0 + jnp.arange(block_row_count, dtype=jnp.int32)[:, None]
    key_pos = (
        first_pos
        + 0
        - WINDOW_KEYS
        + jnp.arange(block_row_count + WINDOW_KEYS, dtype=jnp.int32)[None, :]
    )
    inside = (key_pos <= query_pos) & (key_pos > query_pos - WINDOW_KEYS) & (key_pos >= 0)
    mixed = attend(
        query_block,
        keys_all[..., :head_dim],
        keys_all[..., head_dim:],
        inside,
        sink_row_block,
        factor,
    )
    outputs = mixed.reshape(block_row_count, q_heads * head_dim)
    head_partial = jnp.dot(
        outputs,
        lax.all_gather(out_proj, "ctx", axis=1, tiled=True),
        preferred_element_type=jnp.float32,
    )
    d_model = head_partial.shape[1]
    residual = hidden_in.astype(jnp.float32) + lax.psum_scatter(
        head_partial.astype(jnp.bfloat16), "tp", scatter_dimension=1, tiled=True
    ).astype(jnp.float32)
    square_total = lax.psum(jnp.sum(residual * residual, -1), "tp")
    normed = (residual * lax.rsqrt(square_total[:, None] / d_model + 1e-05) * norm_gain).astype(
        jnp.bfloat16
    )
    ctx_count = lax.axis_size("ctx")
    tp_count = lax.axis_size("tp")
    top_count = routes.shape[1]
    experts = ctx_count * expert_in.shape[0]
    capacity = max(2, min(tok_rows, 3 * top_count * tok_rows // experts))
    quarter_w = d_model // tp_count
    onehot = (routes[:, :, None] == jnp.arange(experts, dtype=jnp.int32)).astype(jnp.int32)
    per_tok = jnp.sum(onehot, 1)
    before = jnp.cumsum(per_tok, axis=0) - per_tok
    slot_ids = jnp.sum(onehot * before[:, None, :], -1)
    flat_index = (routes * capacity + slot_ids).reshape(-1)
    weights = route_scores / jnp.sum(route_scores, -1, keepdims=True)
    full_data = lax.all_gather(normed, "tp", axis=1, tiled=True)
    row_width = full_data.shape[1]
    spread = jnp.broadcast_to(full_data[:, None, :], (tok_rows, top_count, row_width)).reshape(
        -1, row_width
    )
    outbox = jnp.zeros((experts * capacity, row_width), jnp.bfloat16).at[flat_index].set(spread)
    arrived = lax.all_to_all(
        outbox.reshape(ctx_count, 1, capacity, row_width),
        "ctx",
        split_axis=0,
        concat_axis=1,
        tiled=True,
    )
    leading = arrived.shape[:3]
    row_data = arrived.reshape(-1, d_model)
    gate_vals = jnp.dot(row_data, expert_in[0, 0], preferred_element_type=jnp.float32)
    up_vals = jnp.dot(row_data, expert_in[0, 1], preferred_element_type=jnp.float32)
    activated = ((up_vals + 1.0) * gate_vals * jax.nn.sigmoid(1.702 * gate_vals)).astype(
        jnp.bfloat16
    )
    partial_value = jnp.dot(activated, expert_out[0], preferred_element_type=jnp.float32).astype(
        jnp.bfloat16
    )
    result = partial_value.reshape(leading + (d_model,))
    returned = lax.all_to_all(result, "ctx", split_axis=1, concat_axis=0, tiled=True)
    picked = returned.reshape(-1, d_model)[flat_index].reshape(tok_rows, top_count, d_model)
    expert_result = lax.psum_scatter(
        picked.astype(jnp.float32).astype(jnp.bfloat16), "tp", scatter_dimension=2, tiled=True
    )
    moe_sum = jnp.zeros((tok_rows, quarter_w), jnp.float32)
    for member in range(top_count):
        moe_sum = moe_sum + weights[:, member : member + 1] * expert_result[:, member].astype(
            jnp.float32
        )
    return (residual + moe_sum).astype(jnp.bfloat16)


def solution(mesh):
    in_specs = (
        P("ctx", "tp"),
        P("ctx", "tp"),
        P("ctx", "tp", None),
        P("tp"),
        P("tp", "ctx"),
        P("tp"),
        P("ctx", None, None, "tp"),
        P("ctx", "tp", None),
        P("ctx", None),
        P("ctx", None),
    )
    out_specs = P("ctx", "tp")
    return jax.shard_map(body, mesh=mesh, in_specs=in_specs, out_specs=out_specs, check_vma=False)
```

profile of v0, /device:TPU:1, one launch (start us, length us, event | category | flops | bytes accessed | tf_op | source)
XLA Modules:
  0.0 596.0 jit_solution(12314358451730001000)
XLA Ops:
  6.5 0.7 all-gather.3.cloned.1.call-update
  7.3 0.9 copy.32
  8.2 5.4 collective-permute-start
  13.6 0.1 and_and_fusion
  13.7 1.0 copy.34
  14.8 2.2 collective-permute-done
  17.0 0.3 select_reduce_fusion
  17.3 0.7 broadcast_maximum_fusion
  18.1 0.2 fusion.14
  18.3 0.4 convolution_convert_fusion.2
  18.7 80.7 %all-gather.3.cloned.1.call-done = bf16[128,12,512]{2,1,0:T(8,128)(2,1)} async-done(((bf16[1,12,512]{2,1,0:T(8,128)(2,1)}), bf16[128,12,512]{2,1,0:T(8,128)(2,1)}) %all-gather.3.cloned.1.call-update) | async-done | bytes 1572880 | tf_op jit(solution)/shard_map/all_gather | solution.py:72
  99.4 2.5 reshape.218
  102.0 0.7 convolution_convert_fusion.1
  102.6 0.9 copy.41
  103.6 0.1 convert_reduce_fusion
  103.7 0.2 reduce_window_sum.11
  103.9 0.2 select_reduce_fusion.1
  104.1 0.1 copy.36
  104.3 0.1 reshape.190
  104.4 19.8 %reduce-scatter.7.cloned.1.call-done = bf16[384,128]{1,0:T(8,128)(2,1)} async-done(((bf16[1536,128]{1,0:T(8,128)(2,1)}), bf16[384,128]{1,0:T(8,128)(2,1)}) %reduce-scatter.7.cloned.1.call-update) | async-done | bytes 98320
  124.2 1.0 copy.42
  125.2 0.1 multiply_reduce_fusion
  125.4 6.9 %psum.7 = f32[128]{0:T(128)S(1)} all-reduce(f32[128]{0:T(128)S(1)} %multiply_reduce_fusion), channel_id=1, replica_groups=mesh['ctx'=128,'tp'=4] {'tp'}, use_global_device_ids=true, to_apply=%region_8.9 | all-reduce | flops 128 | bytes 1024 | tf_op jit(solution)/shard_map/psum | solution.py:79
  132.4 10.0 %all_gather.7 = bf16[128,1536]{1,0:T(8,128)(2,1)S(1)} all-gather(bf16[128,384]{1,0:T(8,128)(2,1)S(1)} %multiply_convert_fusion), channel_id=1, replica_groups=mesh['ctx'=128,'tp'=4] {'tp'}, dimensions={1}, use_global_device_ids=true | all-gather | bytes 491520 | tf_op jit(solution)/shard_map/all_gather | solution.py:95
  142.4 0.4 broadcast_in_dim.20
  142.8 1.4 reshape.213
  144.2 6.9 %scatter_custom_fusion = bf16[1536,1536]{1,0:T(8,128)(2,1)} fusion(s32[512]{0:T(512)S(1)} %bitcast.86, bf16[512,1536]{1,0:T(8,128)(2,1)} %reshape.213, bf16[]{:T(256)} %constant.14.clone.1), kind=kCustom, calls=%fused_computation.8 | custom fusion | bytes 4719104 | tf_op jit(solution)/shard_map/scatter | solution.py:100
  151.0 8.1 %reshape.192 = bf16[128,1,12,1536]{3,2,0,1:T(8,128)(2,1)} reshape(bf16[1536,1536]{1,0:T(8,128)(2,1)} %scatter_custom_fusion) | data formatting | bytes 9437184 | tf_op jit(solution)/shard_map/reshape | solution.py:102
  159.1 164.5 %all_to_all.8 = bf16[128,1,12,1536]{3,2,1,0:T(8,128)(2,1)} all-to-all(bf16[128,1,12,1536]{3,2,1,0:T(8,128)(2,1)} %bitcast.77), channel_id=1, replica_groups=mesh['ctx'=128,'tp'=4] {'ctx'}, dimensions={0} | all-to-all | bytes 9437184 | tf_op jit(solution)/shard_map/all_to_all | solution.py:101
  323.6 8.2 %reshape.193 = bf16[1536,1536]{1,0:T(8,128)(2,1)} reshape(bf16[128,1,12,1536]{3,2,1,0:T(8,128)(2,1)} %all_to_all.8) | data formatting | bytes 9437184 | tf_op jit(solution)/shard_map/reshape | solution.py:109
  331.8 6.7 %fusion.7 = f32[1536,384]{1,0:T(8,128)} fusion(bf16[1536,1536]{1,0:T(8,128)(2,1)} %reshape.193, bf16[1,2,1536,384]{3,2,1,0:T(8,128)(2,1)} %param.16), kind=kOutput, calls=%fused_computation.14 | convolution fusion | flops 1811939328 | bytes 8257536 | tf_op jit(solution)/shard_map/dot_general | solution.py:110
  338.5 9.1 %convolution_convert_fusion = bf16[1536,1536]{1,0:T(8,128)(2,1)} fusion(bf16[1,384,1536]{2,1,0:T(8,128)(2,1)S(1)} %copy-done, f32[1536,384]{1,0:T(8,128)} %fusion.7, bf16[1536,1536]{1,0:T(8,128)(2,1)} %reshape.193, bf16[1,2,1536,384]{3,2,1,0:T(8,128)(2,1)} %param.16), kind=kOutput, calls=%fused_computation.2 | convolution fusion | flops 3630956544 | bytes 14155776 | tf_op jit(solution)/shard_map/dot_general | solution.py:115
  347.6 8.1 %reshape.194 = bf16[1,128,12,1536]{3,2,1,0:T(8,128)(2,1)} reshape(bf16[1536,1536]{1,0:T(8,128)(2,1)} %convolution_convert_fusion) | data formatting | bytes 9437184 | tf_op jit(solution)/shard_map/reshape | solution.py:118
  355.6 17.5 %all-to-all-start.1 = ((bf16[1,128,12,1536]{3,2,0,1:T(8,128)(2,1)}), bf16[1,128,12,1536]{3,2,0,1:T(8,128)(2,1)}, u32[]{:S(2)}, u32[]{:S(2)}) async-start(bf16[1,128,12,1536]{3,2,0,1:T(8,128)(2,1)} %bitcast.76), calls=%async_computation.1 | async-start | bytes 12582912 | tf_op jit(solution)/shard_map/all_to_all | solution.py:119
  373.3 153.9 %all-to-all-done.1 = bf16[1,128,12,1536]{3,2,0,1:T(8,128)(2,1)} async-done(((bf16[1,128,12,1536]{3,2,0,1:T(8,128)(2,1)}), bf16[1,128,12,1536]{3,2,0,1:T(8,128)(2,1)}, u32[]{:S(2)}, u32[]{:S(2)}) %all-to-all-start.1) | async-done | bytes 4718624 | tf_op jit(solution)/shard_map/all_to_all | solution.py:119
  527.2 8.2 %reshape.195 = bf16[1536,1536]{1,0:T(8,128)(2,1)} reshape(bf16[1,128,12,1536]{3,2,0,1:T(8,128)(2,1)} %all-to-all-done.1) | data formatting | bytes 9437184 | tf_op jit(solution)/shard_map/reshape | solution.py:120
  535.4 7.4 %gather_fusion = bf16[512,1536]{1,0:T(8,128)(2,1)} fusion(bf16[1536,1536]{1,0:T(8,128)(2,1)} %reshape.195, s32[1024]{0:T(1024)S(1)} %pad_clamp_fusion), kind=kCustom, calls=%fused_computation | custom fusion | bytes 3147776 | tf_op jit(solution)/shard_map/gather | solution.py:120
  542.7 2.9 reshape.196
  545.6 2.4 copy.43
  548.1 2.8 copy.52
  551.0 35.4 %reduce-scatter.9.cloned.1.call-done = bf16[384,512]{1,0:T(8,128)(2,1)} async-done(((bf16[1536,512]{1,0:T(8,128)(2,1)}), bf16[384,512]{1,0:T(8,128)(2,1)}) %reduce-scatter.9.cloned.1.call-update) | async-done | bytes 393232
  586.4 1.1 reshape.224
  587.5 0.6 fusion.32
  588.1 0.1 copy.46
  588.2 0.1 copy.47
  588.4 0.1 copy.48
  588.5 0.1 copy.49
  588.7 0.8 fusion.18
  (32 shorter events, 0.4 us)
Async XLA Ops:
  6.5 332.0 %copy-start = (bf16[1,384,1536]{2,1,0:T(8,128)(2,1)S(1)}, bf16[1,384,1536]{2,1,0:T(8,128)(2,1)}, u32[]{:S(2)}) copy-start(bf16[1,384,1536]{2,1,0:T(8,128)(2,1)} %param.17) | copy-start | bytes 3538948
  6.5 11.7 %copy-start.6 = (f32[8]{0:T(128)S(1)}, f32[8]{0:T(128)}, u32[]{:S(2)}) copy-start(f32[8]{0:T(128)} %param.13) | copy-start | bytes 100
  6.5 92.9 %all-gather.3.cloned.1.call-start = ((), (), s32[]{:S(2)}) async-start(), calls=%async_computation.4 | async-start | bytes 2113536 | tf_op jit(solution)/shard_map/all_gather | solution.py:72
  7.3 117.0 %reduce-scatter.7.cloned.1.call-start = ((), (), s32[]{:S(2)}) async-start(), calls=%async_computation.5 | async-start | bytes 491520
  8.2 8.8 %collective-permute-start = (bf16[128,1,128]{0,2,1:T(8,128)(2,1)S(1)}, bf16[128,1,128]{0,2,1:T(8,128)(2,1)S(1)}, u32[]{:S(2)}, u32[]{:S(2)}) collective-permute-start(bf16[128,1,128]{0,2,1:T(8,128)(2,1)S(1)} %copy.32), channel_id=1, source_target_pairs={{0,4},{4,8},{8,12},{12,16},{16,20},{20,24},{24,28},{28,32},{32,36}... | collective-permute-start | bytes 98312 | tf_op jit(solution)/shard_map/ppermute | solution.py:12
  101.9 1.6 copy-start.3
  101.9 23.3 %copy-start.2 = (bf16[128,384]{1,0:T(8,128)(2,1)S(1)}, bf16[128,384]{1,0:T(8,128)(2,1)}, u32[]{:S(2)}) copy-start(bf16[128,384]{1,0:T(8,128)(2,1)} %param.10) | copy-start | bytes 294916
  101.9 30.3 %copy-start.5 = (f32[384]{0:T(512)S(1)}, f32[384]{0:T(512)}, u32[]{:S(2)}) copy-start(f32[384]{0:T(512)} %param.15) | copy-start | bytes 4612
  355.6 171.5 %all-to-all-start.1 = ((bf16[1,128,12,1536]{3,2,0,1:T(8,128)(2,1)}), bf16[1,128,12,1536]{3,2,0,1:T(8,128)(2,1)}, u32[]{:S(2)}, u32[]{:S(2)}) async-start(bf16[1,128,12,1536]{3,2,0,1:T(8,128)(2,1)} %bitcast.76), calls=%async_computation.1 | async-start | bytes 12582912 | tf_op jit(solution)/shard_map/all_to_all | solution.py:119
  373.2 213.2 %reduce-scatter.9.cloned.1.call-start = ((), (), s32[]{:S(2)}) async-start(), calls=%async_computation.6 | async-start | bytes 1966080
  548.1 2.9 copy-start.4
  550.9 38.5 %copy-start.1 = (bf16[1,384,1536]{2,1,0:T(8,128)(2,1)S(1)}, bf16[1,384,1536]{2,1,0:T(8,128)(2,1)}, u32[]{:S(2)}) copy-start(bf16[1,384,1536]{2,1,0:T(8,128)(2,1)} %param.17) | copy-start | bytes 3538948
Sparse Core Ops, SparseCore 0:
  10.5 88.9 all-gather.2
  103.7 20.4 reduce-scatter.6
  551.1 35.3 reduce-scatter.8
where the time goes:
time: 597 us; the launch traced here: 596 us
  waiting for transfers between devices  293 us (49%)
  blocking collectives  181 us (30%)
  local copies, waits for them, and re-layouts  65.4 us (11%)
  starting transfers between devices  23 us (4%)
  matrix products  17.1 us (3%)
  between operations  13.4 us (2%)
    all_to_all x1, blocking collectives, body(): lax.all_to_all(outbox.reshape(ctx_count, 1, capacity, row_width), 'ctx',...  165 us
    all_to_all x1, waiting for transfers between devices, body(): lax.all_to_all(result, 'ctx', split_axis=1, concat_axis=0, tiled=True)  154 us
    all_gather x1, waiting for transfers between devices, body(): lax.all_gather(out_proj, 'ctx', axis=1, tiled=True)  80.7 us
    unnamed x5, waiting for transfers between devices  56 us
    all_to_all x1, starting transfers between devices, body(): lax.all_to_all(result, 'ctx', split_axis=1, concat_axis=0, tiled=True)  17.5 us
    unnamed x26, local copies, waits for them, and re-layouts  13.2 us
  transfers between devices with their start and end apart: 5, of which 5 were waited for; matrix products, arithmetic and copies ran while one was open for 1% of the time, Pallas kernels for 0%

commit v1 on v0

--- a/solution.py
+++ b/solution.py
@@ -69,7 +69,9 @@
     outputs = mixed.reshape(block_row_count, q_heads * head_dim)
     head_partial = jnp.dot(
         outputs,
-        lax.all_gather(out_proj, "ctx", axis=1, tiled=True),
+        jnp.concatenate(
+            lax.all_to_all(jnp.stack([out_proj] * lax.axis_size("ctx")), "ctx", 0, 0), axis=1
+        ),
         preferred_element_type=jnp.float32,
     )
     d_model = head_partial.shape[1]

time: 597 us -> 578 us (0.968)
  waiting for transfers between devices: 293 us -> 255 us
  starting transfers between devices: 23 us -> 40.8 us
    all_gather x1 -> x0, waiting for transfers between devices: 80.7 us -> none  [body(): lax.all_gather(out_proj, 'ctx', axis=1, tiled=True)]
    all_to_all x0 -> x1, waiting for transfers between devices: none -> 45.9 us  [body(): lax.all_to_all(jnp.stack([out_proj] * lax.axis_size('ctx')), 'ctx', 0, 0)]
    all_to_all x0 -> x1, starting transfers between devices: none -> 18.5 us  [body(): lax.all_to_all(jnp.stack([out_proj] * lax.axis_size('ctx')), 'ctx', 0, 0)]
    unnamed x26 -> x27, local copies, waits for them, and re-layouts: 13.2 us -> 9.98 us
    unnamed x5 -> x4, waiting for transfers between devices: 56 us -> 54.5 us
where the time goes in v1:
time: 578 us; the launch traced here: 577 us
  waiting for transfers between devices  255 us (44%)
  blocking collectives  181 us (31%)
  local copies, waits for them, and re-layouts  66 us (11%)
  starting transfers between devices  40.8 us (7%)
  matrix products  18.5 us (3%)
  between operations  13.7 us (2%)
    all_to_all x1, blocking collectives, body(): lax.all_to_all(outbox.reshape(ctx_count, 1, capacity, row_width), 'ctx',...  164 us
    all_to_all x1, waiting for transfers between devices, body(): lax.all_to_all(result, 'ctx', split_axis=1, concat_axis=0, tiled=True)  154 us
    unnamed x4, waiting for transfers between devices  54.5 us
    all_to_all x1, waiting for transfers between devices, body(): lax.all_to_all(jnp.stack([out_proj] * lax.axis_size('ctx')), 'ctx', 0, 0)  45.9 us
    all_to_all x1, starting transfers between devices, body(): lax.all_to_all(result, 'ctx', split_axis=1, concat_axis=0, tiled=True)  18.7 us
    all_to_all x1, starting transfers between devices, body(): lax.all_to_all(jnp.stack([out_proj] * lax.axis_size('ctx')), 'ctx', 0, 0)  18.5 us
  transfers between devices with their start and end apart: 5, of which 5 were waited for; matrix products, arithmetic and copies ran while one was open for 1% of the time, Pallas kernels for 0%

profile of v1, /device:TPU:1, one launch (start us, length us, event | category | flops | bytes accessed | tf_op | source)
XLA Modules:
  0.0 576.5 jit_solution(10161527481028939329)
XLA Ops:
  6.5 2.4 stack.2
  9.0 18.5 %all-to-all-start = ((bf16[128,512,12]{1,2,0:T(8,128)(2,1)}), bf16[128,512,12]{1,2,0:T(8,128)(2,1)S(1)}, u32[]{:S(2)}, u32[]{:S(2)}) async-start(bf16[128,512,12]{1,2,0:T(8,128)(2,1)} %stack.2), calls=%async_computation | async-start | bytes 4194304 | tf_op jit(solution)/shard_map/all_to_all | solution.py:73
  27.6 0.1 copy.33
  27.7 3.5 collective-permute-start
  31.3 0.1 and_and_fusion
  31.4 1.0 copy.35
  32.5 0.2 collective-permute-done
  32.7 0.3 select_reduce_fusion
  33.1 0.2 fusion.14
  33.3 0.4 convolution_convert_fusion.2
  33.7 45.9 %all-to-all-done = bf16[128,512,12]{1,2,0:T(8,128)(2,1)S(1)} async-done(((bf16[128,512,12]{1,2,0:T(8,128)(2,1)}), bf16[128,512,12]{1,2,0:T(8,128)(2,1)S(1)}, u32[]{:S(2)}, u32[]{:S(2)}) %all-to-all-start) | async-done | bytes 1572896 | tf_op jit(solution)/shard_map/all_to_all | solution.py:73
  79.7 1.3 reshape.199
  81.0 2.1 convolution_convert_fusion.1
  83.1 0.9 copy.42
  84.0 0.1 convert_reduce_fusion
  84.2 0.2 reduce_window_sum.11
  84.4 0.2 select_reduce_fusion.1
  84.6 0.1 copy.37
  84.7 0.1 reshape.200
  84.9 19.0 %reduce-scatter.7.cloned.1.call-done = bf16[384,128]{1,0:T(8,128)(2,1)} async-done(((bf16[1536,128]{1,0:T(8,128)(2,1)}), bf16[384,128]{1,0:T(8,128)(2,1)}) %reduce-scatter.7.cloned.1.call-update) | async-done | bytes 98320
  103.9 1.0 copy.43
  104.9 0.1 multiply_reduce_fusion
  105.0 6.8 %psum.7 = f32[128]{0:T(128)S(1)} all-reduce(f32[128]{0:T(128)S(1)} %multiply_reduce_fusion), channel_id=1, replica_groups=mesh['ctx'=128,'tp'=4] {'tp'}, use_global_device_ids=true, to_apply=%region_8.9 | all-reduce | flops 128 | bytes 1024 | tf_op jit(solution)/shard_map/psum | solution.py:81
  111.9 10.0 %all_gather.3 = bf16[128,1536]{1,0:T(8,128)(2,1)S(1)} all-gather(bf16[128,384]{1,0:T(8,128)(2,1)S(1)} %multiply_convert_fusion), channel_id=1, replica_groups=mesh['ctx'=128,'tp'=4] {'tp'}, dimensions={1}, use_global_device_ids=true | all-gather | bytes 491520 | tf_op jit(solution)/shard_map/all_gather | solution.py:97
  122.0 0.4 broadcast_in_dim.20
  122.4 1.4 reshape.223
  123.8 6.9 %scatter_custom_fusion = bf16[1536,1536]{1,0:T(8,128)(2,1)} fusion(s32[512]{0:T(512)S(1)} %bitcast.86, bf16[512,1536]{1,0:T(8,128)(2,1)} %reshape.223, bf16[]{:T(256)} %constant.14.clone.1), kind=kCustom, calls=%fused_computation.8 | custom fusion | bytes 4719104 | tf_op jit(solution)/shard_map/scatter | solution.py:102
  130.6 8.1 %reshape.202 = bf16[128,1,12,1536]{3,2,0,1:T(8,128)(2,1)} reshape(bf16[1536,1536]{1,0:T(8,128)(2,1)} %scatter_custom_fusion) | data formatting | bytes 9437184 | tf_op jit(solution)/shard_map/reshape | solution.py:104
  138.7 164.0 %all_to_all.23 = bf16[128,1,12,1536]{3,2,1,0:T(8,128)(2,1)} all-to-all(bf16[128,1,12,1536]{3,2,1,0:T(8,128)(2,1)} %bitcast.77), channel_id=1, replica_groups=mesh['ctx'=128,'tp'=4] {'ctx'}, dimensions={0} | all-to-all | bytes 9437184 | tf_op jit(solution)/shard_map/all_to_all | solution.py:103
  302.7 8.2 %reshape.203 = bf16[1536,1536]{1,0:T(8,128)(2,1)} reshape(bf16[128,1,12,1536]{3,2,1,0:T(8,128)(2,1)} %all_to_all.23) | data formatting | bytes 9437184 | tf_op jit(solution)/shard_map/reshape | solution.py:111
  310.9 6.7 %fusion.7 = f32[1536,384]{1,0:T(8,128)} fusion(bf16[1536,1536]{1,0:T(8,128)(2,1)} %reshape.203, bf16[1,2,1536,384]{3,2,1,0:T(8,128)(2,1)} %param.16), kind=kOutput, calls=%fused_computation.14 | convolution fusion | flops 1811939328 | bytes 8257536 | tf_op jit(solution)/shard_map/dot_general | solution.py:112
  317.6 9.1 %convolution_convert_fusion = bf16[1536,1536]{1,0:T(8,128)(2,1)} fusion(bf16[1,384,1536]{2,1,0:T(8,128)(2,1)S(1)} %copy-done, f32[1536,384]{1,0:T(8,128)} %fusion.7, bf16[1536,1536]{1,0:T(8,128)(2,1)} %reshape.203, bf16[1,2,1536,384]{3,2,1,0:T(8,128)(2,1)} %param.16), kind=kOutput, calls=%fused_computation.2 | convolution fusion | flops 3630956544 | bytes 14155776 | tf_op jit(solution)/shard_map/dot_general | solution.py:117
  326.6 8.1 %reshape.204 = bf16[1,128,12,1536]{3,2,1,0:T(8,128)(2,1)} reshape(bf16[1536,1536]{1,0:T(8,128)(2,1)} %convolution_convert_fusion) | data formatting | bytes 9437184 | tf_op jit(solution)/shard_map/reshape | solution.py:120
  334.7 18.7 %all-to-all-start.2 = ((bf16[1,128,12,1536]{3,2,0,1:T(8,128)(2,1)}), bf16[1,128,12,1536]{3,2,0,1:T(8,128)(2,1)}, u32[]{:S(2)}, u32[]{:S(2)}) async-start(bf16[1,128,12,1536]{3,2,0,1:T(8,128)(2,1)} %bitcast.76), calls=%async_computation.2 | async-start | bytes 12582912 | tf_op jit(solution)/shard_map/all_to_all | solution.py:121
  353.4 153.9 %all-to-all-done.2 = bf16[1,128,12,1536]{3,2,0,1:T(8,128)(2,1)} async-done(((bf16[1,128,12,1536]{3,2,0,1:T(8,128)(2,1)}), bf16[1,128,12,1536]{3,2,0,1:T(8,128)(2,1)}, u32[]{:S(2)}, u32[]{:S(2)}) %all-to-all-start.2) | async-done | bytes 4718624 | tf_op jit(solution)/shard_map/all_to_all | solution.py:121
  507.3 8.2 %reshape.205 = bf16[1536,1536]{1,0:T(8,128)(2,1)} reshape(bf16[1,128,12,1536]{3,2,0,1:T(8,128)(2,1)} %all-to-all-done.2) | data formatting | bytes 9437184 | tf_op jit(solution)/shard_map/reshape | solution.py:122
  515.6 7.4 %gather_fusion = bf16[512,1536]{1,0:T(8,128)(2,1)} fusion(bf16[1536,1536]{1,0:T(8,128)(2,1)} %reshape.205, s32[1024]{0:T(1024)S(1)} %pad_clamp_fusion), kind=kCustom, calls=%fused_computation | custom fusion | bytes 3147776 | tf_op jit(solution)/shard_map/gather | solution.py:122
  522.9 2.9 reshape.206
  525.8 2.4 copy.44
  528.2 2.8 copy.53
  531.2 35.5 %reduce-scatter.9.cloned.1.call-done = bf16[384,512]{1,0:T(8,128)(2,1)} async-done(((bf16[1536,512]{1,0:T(8,128)(2,1)}), bf16[384,512]{1,0:T(8,128)(2,1)}) %reduce-scatter.9.cloned.1.call-update) | async-done | bytes 393232
  566.6 1.1 reshape.232
  567.7 0.6 fusion.32
  568.3 0.1 copy.47
  568.4 0.1 copy.48
  568.6 0.1 copy.49
  568.7 0.1 copy.50
  568.9 0.8 fusion.18
  (34 shorter events, 0.5 us)
Async XLA Ops:
  6.5 311.1 %copy-start = (bf16[1,384,1536]{2,1,0:T(8,128)(2,1)S(1)}, bf16[1,384,1536]{2,1,0:T(8,128)(2,1)}, u32[]{:S(2)}) copy-start(bf16[1,384,1536]{2,1,0:T(8,128)(2,1)} %param.17) | copy-start | bytes 3538948
  9.0 18.6 %copy-start.3 = (bf16[128,1,128]{2,0,1:T(8,128)(2,1)S(1)}, bf16[128,1,128]{2,0,1:T(8,128)(2,1)}, u32[]{:S(2)}) copy-start(bf16[128,1,128]{2,0,1:T(8,128)(2,1)} %param.12) | copy-start | bytes 98308
  9.0 24.0 %copy-start.7 = (f32[8]{0:T(128)S(1)}, f32[8]{0:T(128)}, u32[]{:S(2)}) copy-start(f32[8]{0:T(128)} %param.13) | copy-start | bytes 100
  9.0 70.7 %all-to-all-start = ((bf16[128,512,12]{1,2,0:T(8,128)(2,1)}), bf16[128,512,12]{1,2,0:T(8,128)(2,1)S(1)}, u32[]{:S(2)}, u32[]{:S(2)}) async-start(bf16[128,512,12]{1,2,0:T(8,128)(2,1)} %stack.2), calls=%async_computation | async-start | bytes 4194304 | tf_op jit(solution)/shard_map/all_to_all | solution.py:73
  27.5 76.3 %reduce-scatter.7.cloned.1.call-start = ((), (), s32[]{:S(2)}) async-start(), calls=%async_computation.5 | async-start | bytes 491520
  27.7 5.0 collective-permute-start
  81.0 3.0 copy-start.4
  81.0 23.9 %copy-start.2 = (bf16[128,384]{1,0:T(8,128)(2,1)S(1)}, bf16[128,384]{1,0:T(8,128)(2,1)}, u32[]{:S(2)}) copy-start(bf16[128,384]{1,0:T(8,128)(2,1)} %param.10) | copy-start | bytes 294916
  81.0 30.9 %copy-start.6 = (f32[384]{0:T(512)S(1)}, f32[384]{0:T(512)}, u32[]{:S(2)}) copy-start(f32[384]{0:T(512)} %param.15) | copy-start | bytes 4612
  334.7 172.6 %all-to-all-start.2 = ((bf16[1,128,12,1536]{3,2,0,1:T(8,128)(2,1)}), bf16[1,128,12,1536]{3,2,0,1:T(8,128)(2,1)}, u32[]{:S(2)}, u32[]{:S(2)}) async-start(bf16[1,128,12,1536]{3,2,0,1:T(8,128)(2,1)} %bitcast.76), calls=%async_computation.2 | async-start | bytes 12582912 | tf_op jit(solution)/shard_map/all_to_all | solution.py:121
  353.4 213.3 %reduce-scatter.9.cloned.1.call-start = ((), (), s32[]{:S(2)}) async-start(), calls=%async_computation.6 | async-start | bytes 1966080
  528.2 2.9 copy-start.5
  531.1 38.6 %copy-start.1 = (bf16[1,384,1536]{2,1,0:T(8,128)(2,1)S(1)}, bf16[1,384,1536]{2,1,0:T(8,128)(2,1)}, u32[]{:S(2)}) copy-start(bf16[1,384,1536]{2,1,0:T(8,128)(2,1)} %param.17) | copy-start | bytes 3538948
Sparse Core Ops, SparseCore 0:
  84.1 19.6 reduce-scatter.6
  531.2 35.3 reduce-scatter.8
